TPU v7x, 512 devices: a whole 4x8x8 slice. The times are simulated.
512 devices in a mesh: req: 64 (over x, z, core), tp: 8 (over y).
Axes of the slice: x: 4, y: 8, z: 8, core: 2. Of those that a mesh axis runs over, the one named last changes fastest.
Arguments:
- residual_input: bfloat16 [8192, 3584], P('req', 'tp'), may hold values from -6 to 6
- new_token_queries: bfloat16 [8192, 4096], P('req', 'tp'), may hold values from -8 to 8
- new_token_keys: bfloat16 [8192, 2048], P('req', 'tp'), may hold values from -8 to 8
- new_token_values: bfloat16 [8192, 2048], P('req', 'tp'), may hold values from -6 to 6
- key_page_pool: bfloat16 [1536, 16, 2048], P('req', None, 'tp'), may hold values from -6 to 6
- value_page_pool: bfloat16 [1536, 16, 2048], P('req', None, 'tp'), may hold values from -6 to 6
- request_page_table: int32 [128, 64], P('req'), may hold values from -1 to 23, as said below
- page_token_length: int32 [128, 64], P('req'), may hold values from 0 to 16, as said below
- request_token_length: int32 [64, 2], P('req'), may hold values from 1 to 96, 128 in all within a row
- request_adapter: int32 [64, 2], P('req'), may hold values from 0 to 63
- adapter_table_row: int32 [64], replicated, may hold values from 0 to 63, each once
- output_weight: bfloat16 [4096, 3584], P('tp'), may hold values from -0.125 to 0.125
- adapter_down_weight: bfloat16 [64, 16, 4096], P('req', None, 'tp'), may hold values from -0.09375 to 0.09375
- adapter_up_weight: bfloat16 [64, 16, 3584], P('req', None, 'tp'), may hold values from -1.5 to 1.5
- norm_scale_row: float32 [3584], P('tp'), may hold values from 0.25 to 1.75
Outputs:
- hidden_out: bfloat16 [8192, 3584], P('req', 'tp')
Inputs may be any that keep to these rules, and one draw needn't show every extreme that they name: request_page_table[q, o] is a page of the pool of owner o (rows o * 24 to o * 24 + 23 of the pools), or -1; so the 2 requests of one index of req take at most 2 pages from one owner, and in every draw the requests of some index of req each take a page from every owner. Requests may share pages. `page_token_length`: 0 exactly where request_page_table is -1; every used page of a request is full but at most one.
All inputs are finite; a program needn't handle non-finite values.
Results may differ from a plain program's by a relative error of at most 0.015.
Values may be sent and summed in bfloat16 or wider, within the bound.
No kernel may reach another device: no remote copies, remote signals or barrier semaphores. Data moves between devices by JAX's collectives and lax.ppermute only.
A program may use at most 64 MiB of HBM per device.

v0:
```python
import jax
import jax.numpy as jnp
from jax import lax
from jax.sharding import PartitionSpec as P

HEAD_SIZE = 256
epsilon = 1e-06
adapter_scale = 2.0
masked_score = -1e30


def attend(query_rows, new_keys, new_values, gathered_keys, gathered_values, usable, owner_request):
    token_count = query_rows.shape[0]
    kv_heads = new_keys.shape[1] // HEAD_SIZE
    group_size = query_rows.shape[1] // new_keys.shape[1]
    requests_here = gathered_keys.shape[0]
    cached_count = gathered_keys.shape[1]
    query_heads = query_rows.reshape(token_count, kv_heads, group_size, HEAD_SIZE)
    past_keys = gathered_keys.reshape(requests_here, cached_count, kv_heads, HEAD_SIZE)
    past_values = gathered_values.reshape(requests_here * cached_count, kv_heads, HEAD_SIZE)
    fresh_keys = new_keys.reshape(token_count, kv_heads, HEAD_SIZE)
    fresh_values = new_values.reshape(token_count, kv_heads, HEAD_SIZE)
    positions = jnp.arange(token_count, dtype=jnp.int32)
    scaling = HEAD_SIZE ** (-0.5)
    past_scores = (
        jnp.einsum("tgqd,rngd->tgqrn", query_heads, past_keys, preferred_element_type=jnp.float32)
        * scaling
    )
    past_mask = usable[None, :, :] & (
        owner_request[:, None, None] == jnp.arange(requests_here, dtype=jnp.int32)[None, :, None]
    )
    past_scores = jnp.where(past_mask[:, None, None, :, :], past_scores, masked_score)
    past_scores = past_scores.reshape(
        token_count, kv_heads, group_size, requests_here * cached_count
    )
    fresh_scores = (
        jnp.einsum("tgqd,ugd->tgqu", query_heads, fresh_keys, preferred_element_type=jnp.float32)
        * scaling
    )
    fresh_mask = (owner_request[:, None] == owner_request[None, :]) & (
        positions[None, :] <= positions[:, None]
    )
    fresh_scores = jnp.where(fresh_mask[:, None, None, :], fresh_scores, masked_score)
    scores = jnp.concatenate([past_scores, fresh_scores], axis=3)
    highest = jnp.max(scores, axis=3, keepdims=True)
    weights = jnp.exp(scores - highest)
    weights = (weights / jnp.sum(weights, axis=3, keepdims=True)).astype(jnp.bfloat16)
    all_values = jnp.concatenate([past_values, fresh_values], axis=0)
    mixed = jnp.einsum("tgqk,kgd->tgqd", weights, all_values, preferred_element_type=jnp.float32)
    return mixed.reshape(token_count, -1).astype(jnp.bfloat16)


def local(
    residual_input,
    new_token_queries,
    new_token_keys,
    new_token_values,
    key_page_pool,
    value_page_pool,
    request_page_table,
    page_token_length,
    request_token_length,
    request_adapter,
    adapter_table_row,
    output_weight,
    adapter_down_weight,
    adapter_up_weight,
    norm_scale_row,
):
    owners = lax.axis_size("req")
    groups = lax.axis_size("tp")
    requests_here = request_page_table.shape[0]
    page_rows = key_page_pool.shape[1]
    token_count = new_token_queries.shape[0]
    width_part = residual_input.shape[1]
    head_cols = key_page_pool.shape[2]
    down_cols = adapter_down_weight.shape[2]
    adapter_pair = jnp.concatenate([adapter_down_weight, adapter_up_weight], axis=2)
    adapters_everywhere = lax.all_gather(adapter_pair, "req", axis=0, tiled=True)
    wanted = lax.all_to_all(request_page_table, "req", split_axis=1, concat_axis=1, tiled=True)
    page_picks = jnp.maximum(wanted, 0)
    kv_pool = jnp.concatenate([key_page_pool, value_page_pool], axis=2)
    kv_out = kv_pool[page_picks]
    kv_back = lax.all_to_all(kv_out, "req", split_axis=1, concat_axis=1, tiled=True)
    kv_back = kv_back.reshape(requests_here, owners * page_rows, 2 * head_cols)
    gathered_keys = kv_back[:, :, :head_cols]
    gathered_values = kv_back[:, :, head_cols:]
    usable = (
        jnp.arange(page_rows, dtype=jnp.int32)[None, None, :] < page_token_length[:, :, None]
    ).reshape(requests_here, owners * page_rows)
    lengths = request_token_length[0]
    positions = jnp.arange(token_count, dtype=jnp.int32)
    ends = jnp.cumsum(lengths)
    owner_request = jnp.sum((positions[:, None] >= ends[None, :]).astype(jnp.int32), axis=1)
    attention = attend(
        new_token_queries,
        new_token_keys,
        new_token_values,
        gathered_keys,
        gathered_values,
        usable,
        owner_request,
    )
    adapters_all = adapter_table_row.shape[0]
    matches = request_adapter[0][:, None] == jnp.arange(adapters_all, dtype=jnp.int32)[None, :]
    chosen_pages = jnp.sum(jnp.where(matches, adapter_table_row[None, :], 0), axis=1)
    rows_here = adapters_everywhere.shape[0]
    picker = (chosen_pages[:, None] == jnp.arange(rows_here, dtype=jnp.int32)[None, :]).astype(
        jnp.bfloat16
    )
    selected = jnp.einsum(
        "rk,kab->rab", picker, adapters_everywhere, preferred_element_type=jnp.float32
    ).astype(jnp.bfloat16)
    adapter_in = selected[:, :, :down_cols]
    adapter_out = selected[:, :, down_cols:]
    rank_size = adapter_in.shape[1]
    selector = (
        owner_request[:, None] == jnp.arange(requests_here, dtype=jnp.int32)[None, :]
    ).astype(jnp.float32)
    selector_half = selector.astype(jnp.bfloat16)
    base_part = jnp.dot(attention, output_weight, preferred_element_type=jnp.float32)
    low_terms = jnp.einsum("tc,rkc->trk", attention, adapter_in, preferred_element_type=jnp.float32)
    low_part = jnp.sum(low_terms * selector[:, :, None], axis=1)
    base_slots = base_part.astype(jnp.bfloat16).reshape(token_count, groups, width_part)
    base_slots = jnp.transpose(base_slots, (1, 0, 2))
    low_slots = jnp.broadcast_to(
        low_part.astype(jnp.bfloat16)[None], (groups, token_count, rank_size)
    )
    pad_cols = -(width_part + rank_size) % 128
    slots = jnp.concatenate(
        [base_slots, low_slots, jnp.zeros((groups, token_count, pad_cols), jnp.bfloat16)], axis=2
    )
    arrived = lax.all_to_all(slots, "tp", split_axis=0, concat_axis=0, tiled=True)
    arrived = arrived.astype(jnp.float32)
    base_local = jnp.sum(arrived[:, :, :width_part], axis=0)
    low_sum = jnp.sum(arrived[:, :, width_part : width_part + rank_size], axis=0)
    rows_masked = (low_sum.astype(jnp.bfloat16)[:, None, :] * selector_half[:, :, None]).reshape(
        token_count, requests_here * rank_size
    )
    projected = base_local + adapter_scale * jnp.dot(
        rows_masked,
        adapter_out.reshape(requests_here * rank_size, width_part),
        preferred_element_type=jnp.float32,
    )
    square_part = jnp.sum(projected * projected, axis=1)
    square_sum = lax.psum(square_part, "tp")
    mean_square = square_sum / (groups * width_part)
    scaled = projected * lax.rsqrt(mean_square + epsilon)[:, None]
    return (residual_input.astype(jnp.float32) + scaled * norm_scale_row).astype(jnp.bfloat16)


def solution(mesh):
    in_specs = (
        P("req", "tp"),
        P("req", "tp"),
        P("req", "tp"),
        P("req", "tp"),
        P("req", None, "tp"),
        P("req", None, "tp"),
        P("req", None),
        P("req", None),
        P("req", None),
        P("req", None),
        P(),
        P("tp", None),
        P("req", None, "tp"),
        P("req", None, "tp"),
        P("tp"),
    )
    out_specs = P("req", "tp")
    return jax.shard_map(local, mesh=mesh, in_specs=in_specs, out_specs=out_specs, check_vma=False)
```

profile of v0, /device:TPU:8, one launch (start us, length us, event | category | flops | bytes accessed | tf_op | source)
XLA Modules:
  0.0 186.8 jit_solution(3870955451242989684)
XLA Ops:
  6.5 0.0 copy-start
  6.5 1.4 copy.88
  8.0 13.8 %all-to-all-start = ((s32[2,64,1]{0,2,1:T(1,128)}), s32[2,64,1]{0,2,1:T(1,128)S(1)}, u32[]{:S(2)}, u32[]{:S(2)}) async-start(s32[2,64,1]{0,2,1:T(1,128)} %copy.88), calls=%async_computation | async-start | bytes 65536 | tf_op jit(solution)/shard_map/all_to_all | solution.py:80
  21.7 0.0 all-gather.2.cloned.1.call-start
  21.8 1.4 pad_maximum_fusion.1
  23.1 0.0 all-gather.2.cloned.1.call-update
  23.2 1.1 pad_maximum_fusion
  24.2 7.0 %all-to-all-done = s32[2,64,1]{0,2,1:T(1,128)S(1)} async-done(((s32[2,64,1]{0,2,1:T(1,128)}), s32[2,64,1]{0,2,1:T(1,128)S(1)}, u32[]{:S(2)}, u32[]{:S(2)}) %all-to-all-start) | async-done | bytes 544 | tf_op jit(solution)/shard_map/all_to_all | solution.py:80
  31.2 0.1 copy.89
  31.3 0.1 reshape.275
  31.4 0.7 gather_fusion
  32.1 1.6 copy.90
  33.7 0.0 copy-start.15
  33.7 0.0 copy-start.12
  33.7 4.8 %all-to-all-start.1 = ((bf16[2,64,16,512]{3,2,0,1:T(8,128)(2,1)}), bf16[2,64,16,512]{3,2,0,1:T(8,128)(2,1)S(1)}, u32[]{:S(2)}, u32[]{:S(2)}) async-start(bf16[2,64,16,512]{3,2,0,1:T(8,128)(2,1)} %copy.90), calls=%async_computation.1 | async-start | bytes 4194304 | tf_op jit(solution)/shard_map/all_to_all | solution.py:84
  38.5 0.0 copy-done.8
  38.5 0.7 copy.92
  39.3 0.0 copy-done.11
  39.3 0.1 lt.27
  39.4 0.1 lt.28
  39.5 0.1 lt.25
  39.6 0.0 copy-done.13
  39.6 0.2 reduce-window.8
  39.7 0.1 pad.2.clone
  39.8 0.1 fusion.30
  39.9 0.0 copy-done.14
  39.9 0.0 copy-done.15
  39.9 0.2 fusion.31
  40.1 0.1 fusion.22
  40.2 0.3 broadcast_and_fusion
  40.6 0.0 copy-done
  40.6 0.9 fusion.38
  41.4 71.5 %all-gather.2.cloned.1.call-done = bf16[64,16,960]{2,1,0:T(8,128)(2,1)} async-done(((bf16[1,16,960]{2,1,0:T(8,128)(2,1)}), bf16[64,16,960]{2,1,0:T(8,128)(2,1)}) %all-gather.2.cloned.1.call-update) | async-done | bytes 1966096 | tf_op jit(solution)/shard_map/all_gather | solution.py:79
  112.9 3.9 %fusion.10 = bf16[2,16,960]{2,0,1:T(2,128)(2,1)S(1)} fusion(bf16[64,16,960]{2,1,0:T(8,128)(2,1)} %all-gather.2.cloned.1.call-done, s32[2]{0:T(128)S(1)} %fusion.31), kind=kOutput, calls=%fused_computation.19 | convolution fusion | flops 3963008 | bytes 2027528 | tf_op jit(solution)/shard_map/rk,kab->rab/dot_general | solution.py:111
  116.8 0.0 all-to-all-done.1
  116.8 0.2 copy.91
  117.0 0.4 copy-done.5
  117.4 1.3 copy-done.1
  118.8 0.1 slice.26
  118.9 1.4 copy.93
  120.3 0.5 copy-done.2
  120.8 1.4 fusion.37
  122.3 0.1 copy.95
  122.4 0.0 copy-start.4
  122.4 0.0 copy-start.9
  122.5 0.7 copy-done.6
  123.2 0.3 fusion.3
  123.5 0.2 copy-done.4
  123.7 0.6 convolution_convert_fusion.1
  124.2 1.5 copy-done.3
  125.7 0.7 convolution_convert_fusion
  126.4 0.6 copy.99
  127.0 0.1 fusion.17
  127.2 1.3 maximum_maximum_fusion
  128.4 6.8 %all-to-all-start.2 = ((bf16[8,128,512]{1,2,0:T(8,128)(2,1)}), bf16[8,128,512]{1,2,0:T(8,128)(2,1)S(1)}, u32[]{:S(2)}, u32[]{:S(2)}) async-start(bf16[8,128,512]{1,2,0:T(8,128)(2,1)} %maximum_maximum_fusion), calls=%async_computation.2 | async-start | bytes 2097152 | tf_op jit(solution)/shard_map/all_to_all | solution.py:133
  135.3 27.7 %all-to-all-done.2 = bf16[8,128,512]{1,2,0:T(8,128)(2,1)S(1)} async-done(((bf16[8,128,512]{1,2,0:T(8,128)(2,1)}), bf16[8,128,512]{1,2,0:T(8,128)(2,1)S(1)}, u32[]{:S(2)}, u32[]{:S(2)}) %all-to-all-start.2) | async-done | bytes 1048608 | tf_op jit(solution)/shard_map/all_to_all | solution.py:133
  162.9 0.1 convert_element_type.79
  163.1 0.0 copy-start.7
  163.1 0.0 copy-start.10
  163.1 0.1 slice_reduce_fusion
  163.2 0.0 slice-done.1
  163.2 0.3 multiply_reduce_fusion
  163.5 15.6 %psum.7 = f32[128]{0:T(128)S(1)} all-reduce(f32[128]{0:T(128)S(1)} %get-tuple-element.12), channel_id=1, replica_groups=mesh['req'=64,'tp'=8] {'tp'}, use_global_device_ids=true, to_apply=%region_10.11 | all-reduce | flops 128 | bytes 1024 | tf_op jit(solution)/shard_map/psum | solution.py:146
  179.1 0.8 add_convert_fusion
  (26 shorter events, 0.1 us)
Async XLA Ops:
  6.5 34.0 %copy-start = (bf16[128,256]{1,0:T(8,128)(2,1)S(1)}, bf16[128,256]{1,0:T(8,128)(2,1)}, u32[]{:S(2)}) copy-start(bf16[128,256]{1,0:T(8,128)(2,1)} %param.17) | copy-start | bytes 196612
  8.0 23.2 %all-to-all-start = ((s32[2,64,1]{0,2,1:T(1,128)}), s32[2,64,1]{0,2,1:T(1,128)S(1)}, u32[]{:S(2)}, u32[]{:S(2)}) async-start(s32[2,64,1]{0,2,1:T(1,128)} %copy.88), calls=%async_computation | async-start | bytes 65536 | tf_op jit(solution)/shard_map/all_to_all | solution.py:80
  21.7 91.2 %all-gather.2.cloned.1.call-start = ((), (), s32[]{:S(2)}) async-start(), calls=%async_computation.3 | async-start | bytes 2129920 | tf_op jit(solution)/shard_map/all_gather | solution.py:79
  33.7 4.9 %copy-start.8 = (bf16[128,256]{1,0:T(8,128)(2,1)S(1)}, bf16[128,256]{1,0:T(8,128)(2,1)}, u32[]{:S(2)}) copy-start(bf16[128,256]{1,0:T(8,128)(2,1)} %param.18) | copy-start | bytes 196612
  33.7 5.6 %copy-start.11 = (s32[2,64]{1,0:T(2,128)S(1)}, s32[2,64]{1,0:T(2,128)}, u32[]{:S(2)}) copy-start(s32[2,64]{1,0:T(2,128)} %param.22) | copy-start | bytes 1540
  33.7 5.9 %copy-start.13 = (s32[1,2]{1,0:T(1,128)S(1)}, s32[1,2]{1,0:T(1,128)}, u32[]{:S(2)}) copy-start(s32[1,2]{1,0:T(1,128)} %param.23) | copy-start | bytes 28
  33.7 6.2 %copy-start.14 = (s32[64]{0:T(128)S(1)}, s32[64]{0:T(128)}, u32[]{:S(2)}) copy-start(s32[64]{0:T(128)} %param.25) | copy-start | bytes 772
  33.7 6.2 %copy-start.15 = (s32[1,2]{1,0:T(1,128)S(1)}, s32[1,2]{1,0:T(1,128)}, u32[]{:S(2)}) copy-start(s32[1,2]{1,0:T(1,128)} %param.24) | copy-start | bytes 28
  33.7 6.9 %copy-start.12 = (bf16[128,512]{1,0:T(8,128)(2,1)S(1)}, bf16[128,512]{1,0:T(8,128)(2,1)}, u32[]{:S(2)}) copy-start(bf16[128,512]{1,0:T(8,128)(2,1)} %param.16) | copy-start | bytes 393220
  33.7 83.1 %all-to-all-start.1 = ((bf16[2,64,16,512]{3,2,0,1:T(8,128)(2,1)}), bf16[2,64,16,512]{3,2,0,1:T(8,128)(2,1)S(1)}, u32[]{:S(2)}, u32[]{:S(2)}) async-start(bf16[2,64,16,512]{3,2,0,1:T(8,128)(2,1)} %copy.90), calls=%async_computation.1 | async-start | bytes 4194304 | tf_op jit(solution)/shard_map/all_to_all | solution.py:84
  116.8 0.6 copy-start.5
  117.4 1.3 copy-start.1
  118.8 2.0 %copy-start.2 = (bf16[2,64,16,512]{3,2,1,0:T(8,128)(2,1)S(1)}, bf16[2,64,16,512]{3,2,1,0:T(8,128)(2,1)}, u32[]{:S(2)}) copy-start(bf16[2,64,16,512]{3,2,1,0:T(8,128)(2,1)} %copy-done.1) | copy-start | bytes 6291460
  122.3 0.9 copy-start.6
  122.4 1.2 copy-start.4
  122.4 1.2 copy-start.9
  123.7 2.0 %copy-start.3 = (bf16[512,3584]{1,0:T(8,128)(2,1)S(1)}, bf16[512,3584]{1,0:T(8,128)(2,1)}, u32[]{:S(2)}) copy-start(bf16[512,3584]{1,0:T(8,128)(2,1)} %param.26) | copy-start | bytes 11010052
  125.7 1.3 slice-start
  128.4 34.5 %all-to-all-start.2 = ((bf16[8,128,512]{1,2,0:T(8,128)(2,1)}), bf16[8,128,512]{1,2,0:T(8,128)(2,1)S(1)}, u32[]{:S(2)}, u32[]{:S(2)}) async-start(bf16[8,128,512]{1,2,0:T(8,128)(2,1)} %maximum_maximum_fusion), calls=%async_computation.2 | async-start | bytes 2097152 | tf_op jit(solution)/shard_map/all_to_all | solution.py:133
  135.3 27.9 %slice-start.1 = ((bf16[2,16,960]{2,0,1:T(2,128)(2,1)}), bf16[2,16,448]{2,0,1:T(2,128)(2,1)S(1)}, s32[]{:S(2)}) async-start(bf16[2,16,960]{2,0,1:T(2,128)(2,1)} %copy-done.5), calls=%async_computation.5 | async-start | bytes 65536 | tf_op jit(solution)/shard_map/slice | solution.py:115
  163.1 16.1 %copy-start.7 = (bf16[128,448]{0,1:T(8,128)(2,1)S(1)}, bf16[128,448]{0,1:T(8,128)(2,1)}, u32[]{:S(2)}) copy-start(bf16[128,448]{0,1:T(8,128)(2,1)} %param.15) | copy-start | bytes 344068
  163.1 16.1 %copy-start.10 = (f32[448]{0:T(512)S(1)}, f32[448]{0:T(512)}, u32[]{:S(2)}) copy-start(f32[448]{0:T(512)} %param.29) | copy-start | bytes 5380
Sparse Core Ops, SparseCore 0:
  25.9 86.9 all-gather.1
where the time goes:
time: 187 us
  waiting for transfers between devices  106 us (57%)
  starting transfers between devices  25.5 us (14%)
  blocking collectives  15.6 us (8%)
  between operations  13.7 us (7%)
  local copies, waits for them, and re-layouts  12.1 us (6%)
  matrix products  7.86 us (4%)
  other arithmetic  5.9 us (3%)
    all_gather x1, waiting for transfers between devices, local(): lax.all_gather(adapter_pair, 'req', axis=0, tiled=True)  71.5 us
    all_to_all x1, waiting for transfers between devices, local(): lax.all_to_all(slots, 'tp', split_axis=0, concat_axis=0, tiled=True)  27.7 us
    psum x1, blocking collectives, local(): square_sum = lax.psum(square_part, 'tp')  15.6 us
    all_to_all x1, starting transfers between devices, local(): lax.all_to_all(request_page_table, 'req', split_axis=1, concat_axis=1, ti...  13.8 us
    all_to_all x1, waiting for transfers between devices, local(): lax.all_to_all(request_page_table, 'req', split_axis=1, concat_axis=1, ti...  6.97 us
    all_to_all x1, starting transfers between devices, local(): lax.all_to_all(slots, 'tp', split_axis=0, concat_axis=0, tiled=True)  6.83 us
    unnamed x33, local copies, waits for them, and re-layouts  5.44 us
    all_to_all x1, starting transfers between devices, local(): lax.all_to_all(kv_out, 'req', split_axis=1, concat_axis=1, tiled=True)  4.84 us
  transfers between devices with their start and end apart: 4, of which 3 were waited for; matrix products, arithmetic and copies ran while one was open for 6% of the time, Pallas kernels for 0%

commit v1 on v0

--- a/solution.py
+++ b/solution.py
@@ -143,7 +143,11 @@
         preferred_element_type=jnp.float32,
     )
     square_part = jnp.sum(projected * projected, axis=1)
-    square_sum = lax.psum(square_part, "tp")
+    square_sum = square_part
+    for hop in (1, 2, 4):
+        square_sum = square_sum + lax.ppermute(
+            square_sum, "tp", [(dev, dev ^ hop) for dev in range(8)]
+        )
     mean_square = square_sum / (groups * width_part)
     scaled = projected * lax.rsqrt(mean_square + epsilon)[:, None]
     return (residual_input.astype(jnp.float32) + scaled * norm_scale_row).astype(jnp.bfloat16)

time: 187 us -> 193 us (1.032)
  the two profiles are of different devices: /device:TPU:8 before, /device:TPU:4 now
where the time goes in v1:
time: 193 us
  waiting for transfers between devices  119 us (62%)
  starting transfers between devices  34.3 us (18%)
  between operations  13.7 us (7%)
  local copies, waits for them, and re-layouts  12.1 us (6%)
  matrix products  7.86 us (4%)
  other arithmetic  5.89 us (3%)
    all_gather x1, waiting for transfers between devices, local(): lax.all_gather(adapter_pair, 'req', axis=0, tiled=True)  70.1 us
    all_to_all x1, waiting for transfers between devices, local(): lax.all_to_all(slots, 'tp', split_axis=0, concat_axis=0, tiled=True)  29.2 us
    ppermute x3, waiting for transfers between devices, local(): lax.ppermute(square_sum, 'tp', [(dev, dev ^ hop) for dev in range(8)])  14.2 us
    all_to_all x1, starting transfers between devices, local(): lax.all_to_all(request_page_table, 'req', split_axis=1, concat_axis=1, ti...  13.9 us
    ppermute x3, starting transfers between devices, local(): lax.ppermute(square_sum, 'tp', [(dev, dev ^ hop) for dev in range(8)])  6.99 us
    all_to_all x1, starting transfers between devices, local(): lax.all_to_all(slots, 'tp', split_axis=0, concat_axis=0, tiled=True)  6.72 us
    all_to_all x1, starting transfers between devices, local(): lax.all_to_all(kv_out, 'req', split_axis=1, concat_axis=1, tiled=True)  6.64 us
    unnamed x33, local copies, waits for them, and re-layouts  5.44 us
  transfers between devices with their start and end apart: 7, of which 6 were waited for; matrix products, arithmetic and copies ran while one was open for 6% of the time, Pallas kernels for 0%

profile of v1, /device:TPU:4, one launch (start us, length us, event | category | flops | bytes accessed | tf_op | source)
XLA Modules:
  0.0 192.5 jit_solution(12697119440369508188)
XLA Ops:
  6.5 1.4 copy.88
  8.0 13.9 %all-to-all-start = ((s32[2,64,1]{0,2,1:T(1,128)}), s32[2,64,1]{0,2,1:T(1,128)S(1)}, u32[]{:S(2)}, u32[]{:S(2)}) async-start(s32[2,64,1]{0,2,1:T(1,128)} %copy.88), calls=%async_computation | async-start | bytes 65536 | tf_op jit(solution)/shard_map/all_to_all | solution.py:80
  21.9 0.0 all-gather.2.cloned.1.call-start
  21.9 1.4 pad_maximum_fusion.1
  23.3 0.0 all-gather.2.cloned.1.call-update
  23.3 1.1 pad_maximum_fusion
  24.4 5.2 %all-to-all-done = s32[2,64,1]{0,2,1:T(1,128)S(1)} async-done(((s32[2,64,1]{0,2,1:T(1,128)}), s32[2,64,1]{0,2,1:T(1,128)S(1)}, u32[]{:S(2)}, u32[]{:S(2)}) %all-to-all-start) | async-done | bytes 544 | tf_op jit(solution)/shard_map/all_to_all | solution.py:80
  29.5 0.1 copy.89
  29.6 0.1 reshape.275
  29.7 0.7 gather_fusion
  30.4 1.6 copy.90
  32.0 0.0 copy-start.15
  32.0 0.0 copy-start.12
  32.0 6.6 %all-to-all-start.1 = ((bf16[2,64,16,512]{3,2,0,1:T(8,128)(2,1)}), bf16[2,64,16,512]{3,2,0,1:T(8,128)(2,1)S(1)}, u32[]{:S(2)}, u32[]{:S(2)}) async-start(bf16[2,64,16,512]{3,2,0,1:T(8,128)(2,1)} %copy.90), calls=%async_computation.1 | async-start | bytes 4194304 | tf_op jit(solution)/shard_map/all_to_all | solution.py:84
  38.7 0.7 copy.92
  39.4 0.1 lt.27
  39.5 0.1 lt.28
  39.6 0.1 lt.25
  39.7 0.2 reduce-window.8
  39.9 0.1 pad.2.clone
  40.0 0.1 fusion.30
  40.1 0.0 copy-done.15
  40.1 0.2 fusion.31
  40.3 0.1 fusion.22
  40.4 0.3 broadcast_and_fusion
  40.7 0.0 copy-done
  40.7 0.0 copy-done.12
  40.7 0.8 fusion.38
  41.6 70.1 %all-gather.2.cloned.1.call-done = bf16[64,16,960]{2,1,0:T(8,128)(2,1)} async-done(((bf16[1,16,960]{2,1,0:T(8,128)(2,1)}), bf16[64,16,960]{2,1,0:T(8,128)(2,1)}) %all-gather.2.cloned.1.call-update) | async-done | bytes 1966096 | tf_op jit(solution)/shard_map/all_gather | solution.py:79
  111.7 3.9 %fusion.10 = bf16[2,16,960]{2,0,1:T(2,128)(2,1)S(1)} fusion(bf16[64,16,960]{2,1,0:T(8,128)(2,1)} %all-gather.2.cloned.1.call-done, s32[2]{0:T(128)S(1)} %fusion.31), kind=kOutput, calls=%fused_computation.19 | convolution fusion | flops 3963008 | bytes 2027528 | tf_op jit(solution)/shard_map/rk,kab->rab/dot_general | solution.py:111
  115.6 0.0 all-to-all-done.1
  115.6 0.2 copy.91
  115.8 0.4 copy-done.5
  116.2 1.4 copy-done.1
  117.6 0.1 slice.26
  117.7 1.4 copy.93
  119.1 0.5 copy-done.2
  119.6 1.5 fusion.37
  121.1 0.1 copy.95
  121.2 0.0 copy-start.9
  121.3 0.7 copy-done.6
  122.0 0.3 fusion.3
  122.3 0.2 copy-done.4
  122.5 0.6 convolution_convert_fusion.1
  123.1 1.5 copy-done.3
  124.5 0.7 convolution_convert_fusion
  125.2 0.6 copy.99
  125.8 0.1 fusion.17
  126.0 1.2 maximum_maximum_fusion
  127.2 6.7 %all-to-all-start.2 = ((bf16[8,128,512]{1,2,0:T(8,128)(2,1)}), bf16[8,128,512]{1,2,0:T(8,128)(2,1)S(1)}, u32[]{:S(2)}, u32[]{:S(2)}) async-start(bf16[8,128,512]{1,2,0:T(8,128)(2,1)} %maximum_maximum_fusion), calls=%async_computation.2 | async-start | bytes 2097152 | tf_op jit(solution)/shard_map/all_to_all | solution.py:133
  134.0 29.2 %all-to-all-done.2 = bf16[8,128,512]{1,2,0:T(8,128)(2,1)S(1)} async-done(((bf16[8,128,512]{1,2,0:T(8,128)(2,1)}), bf16[8,128,512]{1,2,0:T(8,128)(2,1)S(1)}, u32[]{:S(2)}, u32[]{:S(2)}) %all-to-all-start.2) | async-done | bytes 1048608 | tf_op jit(solution)/shard_map/all_to_all | solution.py:133
  163.1 0.1 convert_element_type.79
  163.3 0.0 copy-start.7
  163.3 0.0 copy-start.10
  163.3 0.1 slice_reduce_fusion
  163.4 0.3 multiply_reduce_fusion
  163.7 2.4 %collective-permute-start = (f32[128]{0:T(128)S(1)}, f32[128]{0:T(128)S(1)}, u32[]{:S(2)}, u32[]{:S(2)}) collective-permute-start(f32[128]{0:T(128)S(1)} %get-tuple-element.12), channel_id=1, source_target_pairs={{0,1},{1,0},{2,3},{3,2},{4,5},{5,4},{6,7},{7,6},{8,9},{9,8},{10,11... | collective-permute-start | bytes 1544 | tf_op jit(solution)/shard_map/ppermute | solution.py:148
  166.1 3.0 %collective-permute-done = f32[128]{0:T(128)S(1)} collective-permute-done((f32[128]{0:T(128)S(1)}, f32[128]{0:T(128)S(1)}, u32[]{:S(2)}, u32[]{:S(2)}) %collective-permute-start) | collective-permute-done | bytes 544 | tf_op jit(solution)/shard_map/ppermute | solution.py:148
  169.1 2.1 %collective-permute-start.1 = (f32[128]{0:T(128)S(1)}, f32[128]{0:T(128)S(1)}, u32[]{:S(2)}, u32[]{:S(2)}) collective-permute-start(f32[128]{0:T(128)S(1)} %add.24), channel_id=1, source_target_pairs={{0,2},{1,3},{2,0},{3,1},{4,6},{5,7},{6,4},{7,5},{8,10},{9,11},{10,... | collective-permute-start | bytes 1544 | tf_op jit(solution)/shard_map/ppermute | solution.py:148
  171.3 4.2 %collective-permute-done.1 = f32[128]{0:T(128)S(1)} collective-permute-done((f32[128]{0:T(128)S(1)}, f32[128]{0:T(128)S(1)}, u32[]{:S(2)}, u32[]{:S(2)}) %collective-permute-start.1) | collective-permute-done | bytes 544 | tf_op jit(solution)/shard_map/ppermute | solution.py:148
  175.5 2.4 %collective-permute-start.2 = (f32[128]{0:T(128)S(1)}, f32[128]{0:T(128)S(1)}, u32[]{:S(2)}, u32[]{:S(2)}) collective-permute-start(f32[128]{0:T(128)S(1)} %add.25), channel_id=1, source_target_pairs={{0,4},{1,5},{2,6},{3,7},{4,0},{5,1},{6,2},{7,3},{8,12},{9,13},{10,... | collective-permute-start | bytes 1544 | tf_op jit(solution)/shard_map/ppermute | solution.py:148
  177.9 6.9 %collective-permute-done.2 = f32[128]{0:T(128)S(1)} collective-permute-done((f32[128]{0:T(128)S(1)}, f32[128]{0:T(128)S(1)}, u32[]{:S(2)}, u32[]{:S(2)}) %collective-permute-start.2) | collective-permute-done | bytes 544 | tf_op jit(solution)/shard_map/ppermute | solution.py:148
  184.9 0.0 copy-done.7
  184.9 0.8 add_convert_fusion
  (33 shorter events, 0.1 us)
Async XLA Ops:
  6.5 34.2 %copy-start = (bf16[128,256]{1,0:T(8,128)(2,1)S(1)}, bf16[128,256]{1,0:T(8,128)(2,1)}, u32[]{:S(2)}) copy-start(bf16[128,256]{1,0:T(8,128)(2,1)} %param.17) | copy-start | bytes 196612
  8.0 21.6 %all-to-all-start = ((s32[2,64,1]{0,2,1:T(1,128)}), s32[2,64,1]{0,2,1:T(1,128)S(1)}, u32[]{:S(2)}, u32[]{:S(2)}) async-start(s32[2,64,1]{0,2,1:T(1,128)} %copy.88), calls=%async_computation | async-start | bytes 65536 | tf_op jit(solution)/shard_map/all_to_all | solution.py:80
  21.9 89.8 %all-gather.2.cloned.1.call-start = ((), (), s32[]{:S(2)}) async-start(), calls=%async_computation.3 | async-start | bytes 2129920 | tf_op jit(solution)/shard_map/all_gather | solution.py:79
  32.0 6.7 %copy-start.8 = (bf16[128,256]{1,0:T(8,128)(2,1)S(1)}, bf16[128,256]{1,0:T(8,128)(2,1)}, u32[]{:S(2)}) copy-start(bf16[128,256]{1,0:T(8,128)(2,1)} %param.18) | copy-start | bytes 196612
  32.0 7.4 %copy-start.11 = (s32[2,64]{1,0:T(2,128)S(1)}, s32[2,64]{1,0:T(2,128)}, u32[]{:S(2)}) copy-start(s32[2,64]{1,0:T(2,128)} %param.22) | copy-start | bytes 1540
  32.0 7.7 %copy-start.13 = (s32[1,2]{1,0:T(1,128)S(1)}, s32[1,2]{1,0:T(1,128)}, u32[]{:S(2)}) copy-start(s32[1,2]{1,0:T(1,128)} %param.23) | copy-start | bytes 28
  32.0 8.0 %copy-start.14 = (s32[64]{0:T(128)S(1)}, s32[64]{0:T(128)}, u32[]{:S(2)}) copy-start(s32[64]{0:T(128)} %param.25) | copy-start | bytes 772
  32.0 8.0 %copy-start.15 = (s32[1,2]{1,0:T(1,128)S(1)}, s32[1,2]{1,0:T(1,128)}, u32[]{:S(2)}) copy-start(s32[1,2]{1,0:T(1,128)} %param.24) | copy-start | bytes 28
  32.0 8.7 %copy-start.12 = (bf16[128,512]{1,0:T(8,128)(2,1)S(1)}, bf16[128,512]{1,0:T(8,128)(2,1)}, u32[]{:S(2)}) copy-start(bf16[128,512]{1,0:T(8,128)(2,1)} %param.16) | copy-start | bytes 393220
  32.0 83.6 %all-to-all-start.1 = ((bf16[2,64,16,512]{3,2,0,1:T(8,128)(2,1)}), bf16[2,64,16,512]{3,2,0,1:T(8,128)(2,1)S(1)}, u32[]{:S(2)}, u32[]{:S(2)}) async-start(bf16[2,64,16,512]{3,2,0,1:T(8,128)(2,1)} %copy.90), calls=%async_computation.1 | async-start | bytes 4194304 | tf_op jit(solution)/shard_map/all_to_all | solution.py:84
  115.6 0.6 copy-start.5
  116.2 1.4 copy-start.1
  117.7 2.0 %copy-start.2 = (bf16[2,64,16,512]{3,2,1,0:T(8,128)(2,1)S(1)}, bf16[2,64,16,512]{3,2,1,0:T(8,128)(2,1)}, u32[]{:S(2)}) copy-start(bf16[2,64,16,512]{3,2,1,0:T(8,128)(2,1)} %copy-done.1) | copy-start | bytes 6291460
  121.1 0.9 copy-start.6
  121.2 1.2 copy-start.4
  121.2 1.2 copy-start.9
  122.5 2.0 %copy-start.3 = (bf16[512,3584]{1,0:T(8,128)(2,1)S(1)}, bf16[512,3584]{1,0:T(8,128)(2,1)}, u32[]{:S(2)}) copy-start(bf16[512,3584]{1,0:T(8,128)(2,1)} %param.26) | copy-start | bytes 11010052
  124.5 1.3 slice-start
  127.2 35.9 %all-to-all-start.2 = ((bf16[8,128,512]{1,2,0:T(8,128)(2,1)}), bf16[8,128,512]{1,2,0:T(8,128)(2,1)S(1)}, u32[]{:S(2)}, u32[]{:S(2)}) async-start(bf16[8,128,512]{1,2,0:T(8,128)(2,1)} %maximum_maximum_fusion), calls=%async_computation.2 | async-start | bytes 2097152 | tf_op jit(solution)/shard_map/all_to_all | solution.py:133
  134.0 29.4 %slice-start.1 = ((bf16[2,16,960]{2,0,1:T(2,128)(2,1)}), bf16[2,16,448]{2,0,1:T(2,128)(2,1)S(1)}, s32[]{:S(2)}) async-start(bf16[2,16,960]{2,0,1:T(2,128)(2,1)} %copy-done.5), calls=%async_computation.5 | async-start | bytes 65536 | tf_op jit(solution)/shard_map/slice | solution.py:115
  163.3 21.6 %copy-start.7 = (bf16[128,448]{0,1:T(8,128)(2,1)S(1)}, bf16[128,448]{0,1:T(8,128)(2,1)}, u32[]{:S(2)}) copy-start(bf16[128,448]{0,1:T(8,128)(2,1)} %param.15) | copy-start | bytes 344068
  163.3 21.6 %copy-start.10 = (f32[448]{0:T(512)S(1)}, f32[448]{0:T(512)}, u32[]{:S(2)}) copy-start(f32[448]{0:T(512)} %param.29) | copy-start | bytes 5380
  163.7 5.5 %collective-permute-start = (f32[128]{0:T(128)S(1)}, f32[128]{0:T(128)S(1)}, u32[]{:S(2)}, u32[]{:S(2)}) collective-permute-start(f32[128]{0:T(128)S(1)} %get-tuple-element.12), channel_id=1, source_target_pairs={{0,1},{1,0},{2,3},{3,2},{4,5},{5,4},{6,7},{7,6},{8,9},{9,8},{10,11... | collective-permute-start | bytes 1544 | tf_op jit(solution)/shard_map/ppermute | solution.py:148
  169.1 6.3 %collective-permute-start.1 = (f32[128]{0:T(128)S(1)}, f32[128]{0:T(128)S(1)}, u32[]{:S(2)}, u32[]{:S(2)}) collective-permute-start(f32[128]{0:T(128)S(1)} %add.24), channel_id=1, source_target_pairs={{0,2},{1,3},{2,0},{3,1},{4,6},{5,7},{6,4},{7,5},{8,10},{9,11},{10,... | collective-permute-start | bytes 1544 | tf_op jit(solution)/shard_map/ppermute | solution.py:148
  175.5 9.4 %collective-permute-start.2 = (f32[128]{0:T(128)S(1)}, f32[128]{0:T(128)S(1)}, u32[]{:S(2)}, u32[]{:S(2)}) collective-permute-start(f32[128]{0:T(128)S(1)} %add.25), channel_id=1, source_target_pairs={{0,4},{1,5},{2,6},{3,7},{4,0},{5,1},{6,2},{7,3},{8,12},{9,13},{10,... | collective-permute-start | bytes 1544 | tf_op jit(solution)/shard_map/ppermute | solution.py:148
Sparse Core Ops, SparseCore 0:
  26.1 85.5 all-gather.1
